TPU v7x, 256 devices: a whole 4x4x8 slice. The times are simulated.
256 devices in a mesh: space: 32 (over y_lo, z, core), chan: 8 (over x, y_hi).
Axes of the slice: x: 4, y: 4 (y_hi: 2, y_lo: 2; y = y_hi * 2 + y_lo), z: 8, core: 2. Of those that a mesh axis runs over, the one named last changes fastest.
Arguments:
- inputs: bfloat16 [32, 256, 2048], P('space', 'chan'), may hold values from -6 to 6
- weights: bfloat16 [27, 256, 256], P(None, 'chan'), may hold values from -0.078125 to 0.078125
- cotangent: bfloat16 [32, 256, 2048], P('space', 'chan'), may hold values from -6 to 6
Outputs:
- output: bfloat16 [32, 256, 2048], P('space', 'chan')
- input_grad: bfloat16 [32, 256, 2048], P('space', 'chan')
- weight_grad: float32 [27, 256, 256], P(None, 'chan')
All inputs are finite; a program needn't handle non-finite values.
Results may differ from a plain program's by a relative error of at most 0.001.
Values may be sent and summed in bfloat16 or wider, within the bound.
No kernel may reach another device: no remote copies, remote signals or barrier semaphores. Data moves between devices by JAX's collectives and lax.ppermute only.
A program may use at most 192 MiB of HBM per device.

v0:
```python
import jax
import jax.numpy as jnp
from jax import lax
from jax.sharding import PartitionSpec as P

PLANE_ROWS = 32
ROW_CELLS = 64


def extended(block, sides, width):
    for axis, dim in sides:
        count = lax.axis_size(axis)
        forward = [(i, i + 1) for i in range(count - 1)]
        backward = [(target, source) for source, target in forward]
        low = lax.ppermute(
            lax.slice_in_dim(block, block.shape[dim] - width, None, axis=dim), axis, forward
        )
        high = lax.ppermute(lax.slice_in_dim(block, 0, width, axis=dim), axis, backward)
        block = jnp.concatenate([low, block, high], axis=dim)
    return block


def plane_shift(field, tap_row, tap_col):
    lead = field.shape[:-1]
    grid = field.reshape(lead + (PLANE_ROWS, ROW_CELLS))
    padded = jnp.pad(grid, [(0, 0)] * len(lead) + [(1, 1), (1, 1)])
    window = padded[..., tap_row : tap_row + PLANE_ROWS, tap_col : tap_col + ROW_CELLS]
    return window.reshape(lead + (PLANE_ROWS * ROW_CELLS,))


def stack_at(padded, tap_row, tap_col):
    planes = padded.shape[0] - 2
    moved = plane_shift(padded, tap_row, tap_col)
    return jnp.concatenate(
        [moved[tap_depth : tap_depth + planes] for tap_depth in range(3)], axis=1
    )


def tap_weights(taps, tap_row, tap_col):
    return jnp.concatenate(
        [taps[tap_depth * 9 + tap_row * 3 + tap_col] for tap_depth in range(3)], axis=0
    )


def convolve(padded, taps):
    total = None
    for tap_row in range(3):
        for tap_col in range(3):
            term = jnp.einsum(
                "dcp,co->dop",
                stack_at(padded, tap_row, tap_col),
                tap_weights(taps, tap_row, tap_col),
                preferred_element_type=jnp.float32,
            )
            total = term if total is None else total + term
    return total


def weight_terms(padded, cot_whole, channels):
    pieces = [None] * 27
    for tap_row in range(3):
        for tap_col in range(3):
            block = jnp.einsum(
                "dcp,dop->co",
                stack_at(padded, tap_row, tap_col),
                cot_whole,
                preferred_element_type=jnp.float32,
            )
            block = block.reshape(3, channels, cot_whole.shape[1])
            for tap_depth in range(3):
                pieces[tap_depth * 9 + tap_row * 3 + tap_col] = block[tap_depth]
    return jnp.stack(pieces, axis=0)


def local(inputs, weights, cotangent):
    padded = extended(inputs, (("space", 0),), 1)
    partial_out = convolve(padded, weights)
    output = lax.psum_scatter(partial_out, "chan", scatter_dimension=1, tiled=True).astype(
        jnp.bfloat16
    )
    gathered = lax.all_gather(cotangent, "chan", axis=1, tiled=True)
    cot_padded = extended(gathered, (("space", 0),), 1)
    cot_whole = cot_padded[1:-1]
    flipped = jnp.transpose(weights[::-1], (0, 2, 1))
    input_grad = convolve(cot_padded, flipped).astype(jnp.bfloat16)
    local_terms = weight_terms(padded, cot_whole, inputs.shape[1])
    weight_grad = lax.psum(local_terms, "space")
    return (output, input_grad, weight_grad)


def solution(mesh):
    placed = (P("space", "chan", None), P(None, "chan", None), P("space", "chan", None))
    return jax.shard_map(
        local,
        mesh=mesh,
        in_specs=placed,
        out_specs=(P("space", "chan", None), P("space", "chan", None), P(None, "chan", None)),
        check_vma=False,
    )
```

profile of v0, /device:TPU:1, one launch (start us, length us, event | category | flops | bytes accessed | tf_op | source)
XLA Modules:
  0.0 384.7 jit_solution(320602423577932100)
XLA Ops:
  7.2 5.1 %collective-permute-start.1 = (bf16[1,32,2048]{2,1,0:T(8,128)(2,1)}, bf16[1,32,2048]{2,1,0:T(8,128)(2,1)S(1)}, u32[]{:S(2)}, u32[]{:S(2)}) collective-permute-start(bf16[1,32,2048]{2,1,0:T(8,128)(2,1)} %param.3), channel_id=1, source_target_pairs={{8,0},{16,8},{24,16},{32,24},{40,32},{48,40},{56,48},{64,56},{72,6... | collective-permute-start | bytes 393224 | tf_op jit(solution)/shard_map/ppermute | solution.py:18
  12.3 1.9 collective-permute-start
  14.3 1.5 slice_bitcast_fusion.54
  15.8 1.7 slice_bitcast_fusion.56
  17.5 1.0 reverse_bitcast_fusion
  21.3 0.9 pad_maximum_fusion.1
  23.0 1.5 pad_slice_fusion.25
  24.5 2.8 pad_slice_fusion.26
  27.3 1.3 slice.794
  28.6 1.9 slice.785
  30.5 1.9 slice.787
  32.4 1.9 slice.796
  34.3 1.9 slice.726
  36.2 1.9 slice.792
  38.1 1.9 slice.728
  39.9 1.9 slice.730
  41.8 1.9 slice.735
  43.7 1.9 slice.737
  45.6 1.9 slice.739
  47.4 0.9 slice.744
  48.4 0.9 slice.746
  49.3 0.9 slice.748
  50.2 0.9 slice.753
  55.0 1.5 fusion.76
  60.9 1.8 fusion.45
  62.7 5.0 %all-gather.2.cloned.1.call-done = bf16[1,256,2048]{2,1,0:T(8,128)(2,1)} async-done(((bf16[1,32,2048]{2,1,0:T(8,128)(2,1)}), bf16[1,256,2048]{2,1,0:T(8,128)(2,1)}) %all-gather.2.cloned.1.call-update) | async-done | bytes 1048592 | tf_op jit(solution)/shard_map/all_gather | solution.py:81
  67.7 1.6 copy.7
  69.3 4.3 %collective-permute-start.3 = (bf16[1,256,2048]{1,2,0:T(8,128)(2,1)S(1)}, bf16[1,256,2048]{1,2,0:T(8,128)(2,1)S(1)}, u32[]{:S(2)}, u32[]{:S(2)}) collective-permute-start(bf16[1,256,2048]{1,2,0:T(8,128)(2,1)S(1)} %copy.7), channel_id=1, source_target_pairs={{8,0},{16,8},{24,16},{32,24},{40,32},{48,40},{56,48},{64,56},{72,6... | collective-permute-start | bytes 3145736 | tf_op jit(solution)/shard_map/ppermute | solution.py:18
  73.6 3.1 collective-permute-start.2
  76.7 1.9 fusion.73
  79.2 1.5 fusion.71
  81.4 1.5 fusion.69
  101.3 2.0 pad_maximum_fusion
  103.2 3.5 pad_slice_fusion.1
  106.7 8.9 %pad_slice_fusion.2 = (bf16[1,256,32,64]{1,3,2,0:T(8,128)(2,1)S(1)}, bf16[1,256,32,64]{1,3,2,0:T(8,128)(2,1)}, bf16[1,256,32,64]{1,3,2,0:T(8,128)(2,1)}, bf16[1,...) fusion(bf16[3,256,32,64]{1,3,2,0:T(8,128)(2,1)S(1)} %bitcast.398), kind=kLoop, calls=%fused_computation.94 | loop fusion | bytes 23068672 | tf_op jit(solution)/shard_map/slice | solution.py:35
  115.7 3.0 fusion
  118.9 1.0 fusion.25
  120.8 1.0 fusion.54
  122.6 1.0 fusion.53
  123.7 1.0 fusion.52
  125.0 2.3 fusion.51
  127.3 1.0 fusion.49
  128.9 1.0 fusion.48
  130.4 1.7 fusion.56
  132.1 21.7 %reduce-scatter.2.cloned.1.call-done = f32[1,32,2048]{2,1,0:T(8,128)} async-done(((f32[1,256,2048]{2,1,0:T(8,128)}), f32[1,32,2048]{2,1,0:T(8,128)}) %reduce-scatter.2.cloned.1.call-update) | async-done | bytes 262160 | tf_op jit(solution)/shard_map/reduce_scatter | solution.py:78
  153.7 1.6 convert_element_type.38
  155.3 220.7 %all-reduce.4.cloned.1.call-done = f32[27,32,256]{2,1,0:T(8,128)} async-done(((f32[27,32,256]{2,1,0:T(8,128)}), f32[27,32,256]{2,1,0:T(8,128)}) %all-reduce.4.cloned.1.call-update) | async-done | bytes 884752 | tf_op jit(solution)/shard_map/psum | solution.py:87
  376.0 2.2 copy.38
  (284 shorter events, 33.8 us)
Async XLA Ops:
  7.2 60.5 %all-gather.2.cloned.1.call-start = ((), (), s32[]{:S(2)}) async-start(), calls=%async_computation.2 | async-start | bytes 1179648 | tf_op jit(solution)/shard_map/all_gather | solution.py:81
  7.2 12.8 %collective-permute-start.1 = (bf16[1,32,2048]{2,1,0:T(8,128)(2,1)}, bf16[1,32,2048]{2,1,0:T(8,128)(2,1)S(1)}, u32[]{:S(2)}, u32[]{:S(2)}) collective-permute-start(bf16[1,32,2048]{2,1,0:T(8,128)(2,1)} %param.3), channel_id=1, source_target_pairs={{8,0},{16,8},{24,16},{32,24},{40,32},{48,40},{56,48},{64,56},{72,6... | collective-permute-start | bytes 393224 | tf_op jit(solution)/shard_map/ppermute | solution.py:18
  12.3 7.7 %collective-permute-start = (bf16[1,32,2048]{2,1,0:T(8,128)(2,1)}, bf16[1,32,2048]{2,1,0:T(8,128)(2,1)S(1)}, u32[]{:S(2)}, u32[]{:S(2)}) collective-permute-start(bf16[1,32,2048]{2,1,0:T(8,128)(2,1)} %param.3), channel_id=1, source_target_pairs={{0,8},{8,16},{16,24},{24,32},{32,40},{40,48},{48,56},{56,64},{64,7... | collective-permute-start | bytes 393224 | tf_op jit(solution)/shard_map/ppermute | solution.py:15
  14.3 139.4 %reduce-scatter.2.cloned.1.call-start = ((), (), s32[]{:S(2)}) async-start(), calls=%async_computation.1 | async-start | bytes 2359296 | tf_op jit(solution)/shard_map/reduce_scatter | solution.py:78
  27.3 20.1 %copy-start.11 = (bf16[1,32,32,64]{3,2,1,0:T(8,128)(2,1)S(1)}, bf16[1,32,32,64]{3,2,1,0:T(8,128)(2,1)}, u32[]{:S(2)}) copy-start(bf16[1,32,32,64]{3,2,1,0:T(8,128)(2,1)} %get-tuple-element.33) | copy-start | bytes 393220
  27.3 21.0 %copy-start.10 = (bf16[1,32,32,64]{3,2,1,0:T(8,128)(2,1)S(1)}, bf16[1,32,32,64]{3,2,1,0:T(8,128)(2,1)}, u32[]{:S(2)}) copy-start(bf16[1,32,32,64]{3,2,1,0:T(8,128)(2,1)} %get-tuple-element.34) | copy-start | bytes 393220
  27.3 22.0 %copy-start.9 = (bf16[1,32,32,64]{3,2,1,0:T(8,128)(2,1)S(1)}, bf16[1,32,32,64]{3,2,1,0:T(8,128)(2,1)}, u32[]{:S(2)}) copy-start(bf16[1,32,32,64]{3,2,1,0:T(8,128)(2,1)} %get-tuple-element.35) | copy-start | bytes 393220
  51.2 3.7 copy-start.35
  51.2 3.7 copy-start.40
  52.4 5.3 %copy-start.51 = (bf16[1,32,2048]{2,1,0:T(8,128)(2,1)}, bf16[1,32,2048]{2,1,0:T(8,128)(2,1)S(1)}, u32[]{:S(2)}) copy-start(bf16[1,32,2048]{2,1,0:T(8,128)(2,1)S(1)} %slice.757) | copy-start | bytes 393220
  52.6 3.8 copy-start.27
  52.9 3.5 copy-start.31
  53.2 3.3 copy-start.36
  53.5 5.7 %copy-start.29 = (bf16[1,32,2048]{2,1,0:T(8,128)(2,1)}, bf16[1,32,2048]{2,1,0:T(8,128)(2,1)S(1)}, u32[]{:S(2)}) copy-start(bf16[1,32,2048]{2,1,0:T(8,128)(2,1)S(1)} %slice.774) | copy-start | bytes 393220
  53.5 3.0 copy-start.41
  53.5 3.0 copy-start.45
  53.5 3.0 copy-start.49
  53.8 5.4 %copy-start.33 = (bf16[1,32,2048]{2,1,0:T(8,128)(2,1)}, bf16[1,32,2048]{2,1,0:T(8,128)(2,1)S(1)}, u32[]{:S(2)}) copy-start(bf16[1,32,2048]{2,1,0:T(8,128)(2,1)S(1)} %slice.776) | copy-start | bytes 393220
  54.1 5.1 %copy-start.38 = (bf16[1,32,2048]{2,1,0:T(8,128)(2,1)}, bf16[1,32,2048]{2,1,0:T(8,128)(2,1)S(1)}, u32[]{:S(2)}) copy-start(bf16[1,32,2048]{2,1,0:T(8,128)(2,1)S(1)} %slice.778) | copy-start | bytes 393220
  54.4 5.5 %copy-start.25 = (bf16[1,32,2048]{2,1,0:T(8,128)(2,1)}, bf16[1,32,2048]{2,1,0:T(8,128)(2,1)S(1)}, u32[]{:S(2)}) copy-start(bf16[1,32,2048]{2,1,0:T(8,128)(2,1)S(1)} %slice.783) | copy-start | bytes 393220
  62.6 313.4 %all-reduce.4.cloned.1.call-start = ((), (), s32[]{:S(2)}) async-start(), calls=%async_computation.3 | async-start | bytes 1769472 | tf_op jit(solution)/shard_map/psum | solution.py:87
  67.7 11.6 %copy-start.12 = (bf16[1,256,2048]{2,1,0:T(8,128)(2,1)S(1)}, bf16[1,256,2048]{2,1,0:T(8,128)(2,1)}, u32[]{:S(2)}) copy-start(bf16[1,256,2048]{2,1,0:T(8,128)(2,1)} %all-gather.2.cloned.1.call-done) | copy-start | bytes 3145732
  69.2 14.3 %copy-start.44 = (bf16[1,32,2048]{2,1,0:T(8,128)(2,1)S(1)}, bf16[1,32,2048]{2,1,0:T(8,128)(2,1)}, u32[]{:S(2)}) copy-start(bf16[1,32,2048]{2,1,0:T(8,128)(2,1)} %slice.753) | copy-start | bytes 393220
  69.3 14.3 %copy-start.48 = (bf16[1,32,2048]{2,1,0:T(8,128)(2,1)S(1)}, bf16[1,32,2048]{2,1,0:T(8,128)(2,1)}, u32[]{:S(2)}) copy-start(bf16[1,32,2048]{2,1,0:T(8,128)(2,1)} %slice.755) | copy-start | bytes 393220
  69.3 14.3 %copy-start.52 = (bf16[1,32,2048]{2,1,0:T(8,128)(2,1)S(1)}, bf16[1,32,2048]{2,1,0:T(8,128)(2,1)}, u32[]{:S(2)}) copy-start(bf16[1,32,2048]{2,1,0:T(8,128)(2,1)} %copy-done.51) | copy-start | bytes 393220
  69.3 32.0 %collective-permute-start.3 = (bf16[1,256,2048]{1,2,0:T(8,128)(2,1)S(1)}, bf16[1,256,2048]{1,2,0:T(8,128)(2,1)S(1)}, u32[]{:S(2)}, u32[]{:S(2)}) collective-permute-start(bf16[1,256,2048]{1,2,0:T(8,128)(2,1)S(1)} %copy.7), channel_id=1, source_target_pairs={{8,0},{16,8},{24,16},{32,24},{40,32},{48,40},{56,48},{64,56},{72,6... | collective-permute-start | bytes 3145736 | tf_op jit(solution)/shard_map/ppermute | solution.py:18
  73.6 27.7 %collective-permute-start.2 = (bf16[1,256,2048]{1,2,0:T(8,128)(2,1)S(1)}, bf16[1,256,2048]{1,2,0:T(8,128)(2,1)}, u32[]{:S(2)}, u32[]{:S(2)}) collective-permute-start(bf16[1,256,2048]{1,2,0:T(8,128)(2,1)S(1)} %copy.7), channel_id=1, source_target_pairs={{0,8},{8,16},{16,24},{24,32},{32,40},{40,48},{48,56},{56,64},{64,7... | collective-permute-start | bytes 3145736 | tf_op jit(solution)/shard_map/ppermute | solution.py:15
  78.6 6.1 %copy-start.54 = (bf16[1,32,2048]{2,1,0:T(8,128)(2,1)S(1)}, bf16[1,32,2048]{2,1,0:T(8,128)(2,1)}, u32[]{:S(2)}) copy-start(bf16[1,32,2048]{2,1,0:T(8,128)(2,1)} %param.3) | copy-start | bytes 393220
  78.6 6.1 %copy-start.57 = (bf16[1,32,2048]{2,1,0:T(8,128)(2,1)S(1)}, bf16[1,32,2048]{2,1,0:T(8,128)(2,1)}, u32[]{:S(2)}) copy-start(bf16[1,32,2048]{2,1,0:T(8,128)(2,1)} %copy-done.55) | copy-start | bytes 393220
  78.6 6.0 %copy-start.60 = (bf16[1,32,2048]{2,1,0:T(8,128)(2,1)S(1)}, bf16[1,32,2048]{2,1,0:T(8,128)(2,1)}, u32[]{:S(2)}) copy-start(bf16[1,32,2048]{2,1,0:T(8,128)(2,1)} %copy-done.58) | copy-start | bytes 393220
  80.7 5.0 %copy-start.28 = (bf16[1,32,2048]{2,1,0:T(8,128)(2,1)S(1)}, bf16[1,32,2048]{2,1,0:T(8,128)(2,1)}, u32[]{:S(2)}) copy-start(bf16[1,32,2048]{2,1,0:T(8,128)(2,1)} %copy-done.27) | copy-start | bytes 393220
  80.7 5.0 %copy-start.32 = (bf16[1,32,2048]{2,1,0:T(8,128)(2,1)S(1)}, bf16[1,32,2048]{2,1,0:T(8,128)(2,1)}, u32[]{:S(2)}) copy-start(bf16[1,32,2048]{2,1,0:T(8,128)(2,1)} %copy-done.31) | copy-start | bytes 393220
  80.7 5.0 %copy-start.37 = (bf16[1,32,2048]{2,1,0:T(8,128)(2,1)S(1)}, bf16[1,32,2048]{2,1,0:T(8,128)(2,1)}, u32[]{:S(2)}) copy-start(bf16[1,32,2048]{2,1,0:T(8,128)(2,1)} %copy-done.36) | copy-start | bytes 393220
  82.9 4.0 %copy-start.30 = (bf16[1,32,2048]{2,1,0:T(8,128)(2,1)S(1)}, bf16[1,32,2048]{2,1,0:T(8,128)(2,1)}, u32[]{:S(2)}) copy-start(bf16[1,32,2048]{2,1,0:T(8,128)(2,1)} %copy-done.29) | copy-start | bytes 393220
  82.9 4.0 %copy-start.34 = (bf16[1,32,2048]{2,1,0:T(8,128)(2,1)S(1)}, bf16[1,32,2048]{2,1,0:T(8,128)(2,1)}, u32[]{:S(2)}) copy-start(bf16[1,32,2048]{2,1,0:T(8,128)(2,1)} %copy-done.33) | copy-start | bytes 393220
  82.9 4.0 %copy-start.39 = (bf16[1,32,2048]{2,1,0:T(8,128)(2,1)S(1)}, bf16[1,32,2048]{2,1,0:T(8,128)(2,1)}, u32[]{:S(2)}) copy-start(bf16[1,32,2048]{2,1,0:T(8,128)(2,1)} %copy-done.38) | copy-start | bytes 393220
  84.0 3.9 %copy-start.24 = (bf16[1,32,2048]{2,1,0:T(8,128)(2,1)S(1)}, bf16[1,32,2048]{2,1,0:T(8,128)(2,1)}, u32[]{:S(2)}) copy-start(bf16[1,32,2048]{2,1,0:T(8,128)(2,1)} %slice.787) | copy-start | bytes 393220
  84.0 3.9 %copy-start.26 = (bf16[1,32,2048]{2,1,0:T(8,128)(2,1)S(1)}, bf16[1,32,2048]{2,1,0:T(8,128)(2,1)}, u32[]{:S(2)}) copy-start(bf16[1,32,2048]{2,1,0:T(8,128)(2,1)} %copy-done.25) | copy-start | bytes 393220
  85.1 3.9 %copy-start.22 = (bf16[1,32,2048]{2,1,0:T(8,128)(2,1)S(1)}, bf16[1,32,2048]{2,1,0:T(8,128)(2,1)}, u32[]{:S(2)}) copy-start(bf16[1,32,2048]{2,1,0:T(8,128)(2,1)} %slice.792) | copy-start | bytes 393220
  106.7 8.9 %copy-start.108 = (bf16[256,32]{0,1:T(8,128)(2,1)S(1)}, bf16[256,32]{0,1:T(8,128)(2,1)}, u32[]{:S(2)}) copy-start(bf16[256,32]{0,1:T(8,128)(2,1)} %get-tuple-element.75) | copy-start | bytes 49156
  106.7 8.9 %copy-start.109 = (bf16[256,32]{0,1:T(8,128)(2,1)S(1)}, bf16[256,32]{0,1:T(8,128)(2,1)}, u32[]{:S(2)}) copy-start(bf16[256,32]{0,1:T(8,128)(2,1)} %get-tuple-element.76) | copy-start | bytes 49156
  106.7 8.9 %copy-start.110 = (bf16[256,32]{0,1:T(8,128)(2,1)S(1)}, bf16[256,32]{0,1:T(8,128)(2,1)}, u32[]{:S(2)}) copy-start(bf16[256,32]{0,1:T(8,128)(2,1)} %get-tuple-element.77) | copy-start | bytes 49156
  115.7 3.1 copy-start.6
  115.7 3.1 copy-start.7
  115.7 3.1 copy-start.8
  115.7 3.1 copy-start.100
  115.7 3.1 copy-start.101
  115.7 3.1 copy-start.102
  (70 other events, 103.8 us)
Sparse Core Ops, SparseCore 0:
  14.4 53.2 all-gather.1
  71.7 81.9 reduce-scatter.1
  156.9 219.0 all-reduce.3
where the time goes:
time: 386 us; the launch traced here: 385 us
  waiting for transfers between devices  247 us (64%)
  local copies, waits for them, and re-layouts  75.9 us (20%)
  matrix products  27.2 us (7%)
  between operations  15.1 us (4%)
  starting transfers between devices  14.5 us (4%)
  other arithmetic  4.52 us (1%)
    psum x1, waiting for transfers between devices, local(): weight_grad = lax.psum(local_terms, 'space')  221 us
    slice x28, local copies, waits for them, and re-layouts, stack_at(): moved[tap_depth:tap_depth + planes]  43.6 us
    unnamed x249, local copies, waits for them, and re-layouts  23.8 us
    reduce_scatter x1, waiting for transfers between devices, local(): lax.psum_scatter(partial_out, 'chan', scatter_dimension=1, tiled=True)  21.7 us
    dot_general x18, matrix products, convolve(): jnp.einsum('dcp,co->dop', stack_at(padded, tap_row, tap_col), tap_weights...  19.6 us
    ppermute x2, starting transfers between devices, extended(): lax.ppermute(lax.slice_in_dim(block, 0, width, axis=dim), axis, backward)  9.41 us
  transfers between devices with their start and end apart: 7, of which 3 were waited for; matrix products, arithmetic and copies ran while one was open for 26% of the time, Pallas kernels for 0%

commit v1 on v0

--- a/solution.py
+++ b/solution.py
@@ -17,6 +17,37 @@
         )
         high = lax.ppermute(lax.slice_in_dim(block, 0, width, axis=dim), axis, backward)
         block = jnp.concatenate([low, block, high], axis=dim)
+    return block
+
+
+def partner_masks(count, first):
+    masks = [1 << b for b in range(count.bit_length() - 1)]
+    return [first] + [m for m in masks if m != first]
+
+
+def halving_sum(block, axis, masks, dim):
+    count = lax.axis_size(axis)
+    index = lax.axis_index(axis)
+    for mask in masks:
+        half = block.shape[dim] // 2
+        upper = (index // mask) % 2 == 1
+        low = lax.slice_in_dim(block, 0, half, axis=dim)
+        high = lax.slice_in_dim(block, half, 2 * half, axis=dim)
+        keep = jnp.where(upper, high, low)
+        send = jnp.where(upper, low, high)
+        block = keep + lax.ppermute(send, axis, [(i, i ^ mask) for i in range(count)])
+    return block
+
+
+def doubling_gather(block, axis, masks, dim):
+    count = lax.axis_size(axis)
+    index = lax.axis_index(axis)
+    for mask in masks:
+        upper = (index // mask) % 2 == 1
+        other = lax.ppermute(block, axis, [(i, i ^ mask) for i in range(count)])
+        block = jnp.concatenate(
+            [jnp.where(upper, other, block), jnp.where(upper, block, other)], axis=dim
+        )
     return block
 
 
@@ -75,16 +106,19 @@
 def local(inputs, weights, cotangent):
     padded = extended(inputs, (("space", 0),), 1)
     partial_out = convolve(padded, weights)
-    output = lax.psum_scatter(partial_out, "chan", scatter_dimension=1, tiled=True).astype(
-        jnp.bfloat16
-    )
+    chan_masks = partner_masks(lax.axis_size("chan"), 1)[::-1]
+    output = halving_sum(partial_out, "chan", chan_masks, 1).astype(jnp.bfloat16)
     gathered = lax.all_gather(cotangent, "chan", axis=1, tiled=True)
     cot_padded = extended(gathered, (("space", 0),), 1)
     cot_whole = cot_padded[1:-1]
     flipped = jnp.transpose(weights[::-1], (0, 2, 1))
     input_grad = convolve(cot_padded, flipped).astype(jnp.bfloat16)
     local_terms = weight_terms(padded, cot_whole, inputs.shape[1])
-    weight_grad = lax.psum(local_terms, "space")
+    space_masks = partner_masks(lax.axis_size("space"), 1)
+    space_masks = [space_masks[0], space_masks[-1]] + space_masks[1:-1]
+    flat = local_terms.reshape(-1, local_terms.shape[-1])
+    flat = doubling_gather(halving_sum(flat, "space", space_masks, 0), "space", space_masks[::-1], 0)
+    weight_grad = flat.reshape(local_terms.shape)
     return (output, input_grad, weight_grad)
 
 

time: 386 us -> 202 us (0.52)
  waiting for transfers between devices: 247 us -> 30 us
  starting transfers between devices: 14.5 us -> 63.5 us
  local copies, waits for them, and re-layouts: 75.9 us -> 57 us
    psum x1 -> x0, waiting for transfers between devices: 221 us -> none  [local(): weight_grad = lax.psum(local_terms, 'space')]
    ppermute x0 -> x13, starting transfers between devices: none -> 47.7 us  [the longest x8 36.3 us: halving_sum(): lax.ppermute(send, axis, [(i, i ^ mask) for i in range(count)])]
    ppermute x0 -> x13, waiting for transfers between devices: none -> 25.6 us  [the longest x5 15.4 us: doubling_gather(): other = lax.ppermute(block, axis, [(i, i ^ mask) for i in range(count)])]
    reduce_scatter x1 -> x0, waiting for transfers between devices: 21.7 us -> none  [local(): lax.psum_scatter(partial_out, 'chan', scatter_dimension=1, tiled=True)]
    unnamed x249 -> x194, local copies, waits for them, and re-layouts: 23.8 us -> 6.52 us
  transfers between devices with their start and end apart: 7 -> 18, of which waited for: 3 -> 8; matrix products, arithmetic and copies ran while one was open for 26% -> 42% of each run, Pallas kernels for 0% -> 0%
where the time goes in v1:
time: 202 us; the launch traced here: 201 us
  starting transfers between devices  63.5 us (31%)
  local copies, waits for them, and re-layouts  57 us (28%)
  waiting for transfers between devices  30 us (15%)
  matrix products  27.1 us (13%)
  between operations  15.5 us (8%)
  other arithmetic  7.92 us (4%)
    slice x28, local copies, waits for them, and re-layouts, stack_at(): moved[tap_depth:tap_depth + planes]  44.4 us
    ppermute x8, starting transfers between devices, halving_sum(): lax.ppermute(send, axis, [(i, i ^ mask) for i in range(count)])  36.3 us
    dot_general x18, matrix products, convolve(): jnp.einsum('dcp,co->dop', stack_at(padded, tap_row, tap_col), tap_weights...  18 us
    ppermute x5, waiting for transfers between devices, doubling_gather(): other = lax.ppermute(block, axis, [(i, i ^ mask) for i in range(count)])  15.4 us
    ppermute x2, starting transfers between devices, extended(): lax.ppermute(lax.slice_in_dim(block, 0, width, axis=dim), axis, backward)  11.9 us
    ppermute x5, starting transfers between devices, doubling_gather(): other = lax.ppermute(block, axis, [(i, i ^ mask) for i in range(count)])  11.4 us
    ppermute x8, waiting for transfers between devices, halving_sum(): lax.ppermute(send, axis, [(i, i ^ mask) for i in range(count)])  10.2 us
    dot_general x9, matrix products, weight_terms(): jnp.einsum('dcp,dop->co', stack_at(padded, tap_row, tap_col), cot_whole,...  9.06 us
  transfers between devices with their start and end apart: 18, of which 8 were waited for; matrix products, arithmetic and copies ran while one was open for 42% of the time, Pallas kernels for 0%

profile of v1, /device:TPU:1, one launch (start us, length us, event | category | flops | bytes accessed | tf_op | source)
XLA Modules:
  0.0 200.9 jit_solution(18130266377284447315)
XLA Ops:
  7.2 5.1 %collective-permute-start.1 = (bf16[1,32,2048]{2,1,0:T(8,128)(2,1)}, bf16[1,32,2048]{2,1,0:T(8,128)(2,1)S(1)}, u32[]{:S(2)}, u32[]{:S(2)}) collective-permute-start(bf16[1,32,2048]{2,1,0:T(8,128)(2,1)} %param.3), channel_id=1, source_target_pairs={{8,0},{16,8},{24,16},{32,24},{40,32},{48,40},{56,48},{64,56},{72,6... | collective-permute-start | bytes 393224 | tf_op jit(solution)/shard_map/ppermute | solution.py:18
  12.3 1.9 collective-permute-start
  14.3 1.6 slice_bitcast_fusion.56
  16.0 1.5 slice_bitcast_fusion.54
  20.5 1.5 pad_slice_fusion.25
  22.0 2.8 %pad_slice_fusion.26 = (bf16[1,32,32,64]{3,2,1,0:T(8,128)(2,1)}, bf16[1,32,32,64]{3,2,1,0:T(8,128)(2,1)}, bf16[1,32,32,64]{3,2,1,0:T(8,128)(2,1)}, bf16[1,32,32,...) fusion(bf16[3,32,32,64]{3,2,1,0:T(8,128)(2,1)S(1)} %reshape.285), kind=kLoop, calls=%fused_computation.121 | loop fusion | bytes 2883584 | tf_op jit(solution)/shard_map/slice | solution.py:66
  24.8 1.3 slice.842
  26.1 1.9 slice.833
  28.0 1.9 slice.835
  29.9 1.9 slice.844
  31.8 1.9 slice.774
  33.7 1.9 slice.840
  35.5 1.9 slice.776
  37.4 1.9 slice.778
  39.3 1.9 slice.783
  41.2 1.9 slice.785
  43.1 1.9 slice.787
  52.6 1.5 fusion.76
  54.1 1.5 convolution_add_fusion.6
  60.4 1.1 slice_select_fusion
  61.5 2.5 %collective-permute-start.2 = (f32[1,128,2048]{2,1,0:T(8,128)}, f32[1,128,2048]{2,1,0:T(8,128)}, u32[]{:S(2)}, u32[]{:S(2)}) collective-permute-start(f32[1,128,2048]{2,1,0:T(8,128)} %slice_select_fusion), channel_id=1, source_target_pairs={{0,4},{1,5},{2,6},{3,7},{4,0},{5,1},{6,2},{7,3},{8,12},{9,13},{10,... | collective-permute-start | bytes 3145736 | tf_op jit(solution)/shard_map/ppermute | solution.py:38
  64.0 4.3 %all-gather.2.cloned.1.call-done = bf16[1,256,2048]{2,1,0:T(8,128)(2,1)} async-done(((bf16[1,32,2048]{2,1,0:T(8,128)(2,1)}), bf16[1,256,2048]{2,1,0:T(8,128)(2,1)}) %all-gather.2.cloned.1.call-update) | async-done | bytes 1048592 | tf_op jit(solution)/shard_map/all_gather | solution.py:111
  68.3 1.8 fusion.73
  70.2 1.9 fusion.71
  72.1 1.5 fusion.69
  73.7 1.5 fusion.67
  78.9 22.3 %collective-permute-start.7 = (f32[432,256]{1,0:T(8,128)}, f32[432,256]{1,0:T(8,128)}, u32[]{:S(2)}, u32[]{:S(2)}) collective-permute-start(f32[432,256]{1,0:T(8,128)} %slice_select_fusion.2), channel_id=1, source_target_pairs={{0,8},{8,0},{16,24},{24,16},{32,40},{40,32},{48,56},{56,48},{64,72... | collective-permute-start | bytes 1327112 | tf_op jit(solution)/shard_map/ppermute | solution.py:38
  101.2 1.7 collective-permute-done.7
  102.9 1.1 select_add_fusion.2
  105.1 1.4 select_add_fusion
  106.5 4.2 %collective-permute-done.8 = f32[216,256]{1,0:T(8,128)S(1)} collective-permute-done((f32[216,256]{1,0:T(8,128)S(1)}, f32[216,256]{1,0:T(8,128)S(1)}, u32[]{:S(2)}, u32[]{:S(2)}) %collective-permute-start.8) | collective-permute-done | bytes 221216 | tf_op jit(solution)/shard_map/ppermute | solution.py:38
  110.8 1.4 collective-permute-start.9
  112.4 2.1 %collective-permute-done.9 = f32[108,256]{1,0:T(8,128)S(1)} collective-permute-done((f32[108,256]{1,0:T(8,128)S(1)}, f32[108,256]{1,0:T(8,128)S(1)}, u32[]{:S(2)}, u32[]{:S(2)}) %collective-permute-start.9) | collective-permute-done | bytes 110624 | tf_op jit(solution)/shard_map/ppermute | solution.py:38
  114.6 2.5 %collective-permute-start.10 = (f32[54,256]{1,0:T(8,128)S(1)}, f32[54,256]{1,0:T(8,128)S(1)}, u32[]{:S(2)}, u32[]{:S(2)}) collective-permute-start(f32[54,256]{1,0:T(8,128)S(1)} %slice_select_fusion.6), channel_id=1, source_target_pairs={{0,32},{8,40},{16,48},{24,56},{32,0},{40,8},{48,16},{56,24},{64,96... | collective-permute-start | bytes 165896 | tf_op jit(solution)/shard_map/ppermute | solution.py:38
  118.7 6.3 %collective-permute-start.11 = (f32[27,256]{1,0:T(8,128)S(1)}, f32[27,256]{1,0:T(8,128)S(1)}, u32[]{:S(2)}, u32[]{:S(2)}) collective-permute-start(f32[27,256]{1,0:T(8,128)S(1)} %slice_select_fusion.7), channel_id=1, source_target_pairs={{0,64},{8,72},{16,80},{24,88},{32,96},{40,104},{48,112},{56,120},{... | collective-permute-start | bytes 82952 | tf_op jit(solution)/shard_map/ppermute | solution.py:38
  125.1 1.2 collective-permute-done.11
  126.3 5.5 %collective-permute-start.12 = (f32[27,256]{1,0:T(8,128)S(1)}, f32[27,256]{1,0:T(8,128)S(1)}, u32[]{:S(2)}, u32[]{:S(2)}) collective-permute-start(f32[27,256]{1,0:T(8,128)S(1)} %select_add_fusion.6), channel_id=1, source_target_pairs={{0,64},{8,72},{16,80},{24,88},{32,96},{40,104},{48,112},{56,120},{... | collective-permute-start | bytes 82952 | tf_op jit(solution)/shard_map/ppermute | solution.py:47
  131.9 1.5 copy.7
  133.3 6.8 %collective-permute-start.6 = (bf16[1,256,2048]{1,2,0:T(8,128)(2,1)S(1)}, bf16[1,256,2048]{1,2,0:T(8,128)(2,1)S(1)}, u32[]{:S(2)}, u32[]{:S(2)}) collective-permute-start(bf16[1,256,2048]{1,2,0:T(8,128)(2,1)S(1)} %copy.7), channel_id=1, source_target_pairs={{8,0},{16,8},{24,16},{32,24},{40,32},{48,40},{56,48},{64,56},{72,6... | collective-permute-start | bytes 3145736 | tf_op jit(solution)/shard_map/ppermute | solution.py:18
  140.1 1.9 collective-permute-start.5
  142.1 2.2 %collective-permute-start.13 = (f32[54,256]{1,0:T(8,128)S(1)}, f32[54,256]{1,0:T(8,128)S(1)}, u32[]{:S(2)}, u32[]{:S(2)}) collective-permute-start(f32[54,256]{1,0:T(8,128)S(1)} %pad_maximum_fusion.6), channel_id=1, source_target_pairs={{0,32},{8,40},{16,48},{24,56},{32,0},{40,8},{48,16},{56,24},{64,96... | collective-permute-start | bytes 165896 | tf_op jit(solution)/shard_map/ppermute | solution.py:47
  145.0 10.0 %collective-permute-done.13 = f32[54,256]{1,0:T(8,128)S(1)} collective-permute-done((f32[54,256]{1,0:T(8,128)S(1)}, f32[54,256]{1,0:T(8,128)S(1)}, u32[]{:S(2)}, u32[]{:S(2)}) %collective-permute-start.13) | collective-permute-done | bytes 55328 | tf_op jit(solution)/shard_map/ppermute | solution.py:47
  155.1 2.1 %collective-permute-start.14 = (f32[108,256]{1,0:T(8,128)S(1)}, f32[108,256]{1,0:T(8,128)S(1)}, u32[]{:S(2)}, u32[]{:S(2)}) collective-permute-start(f32[108,256]{1,0:T(8,128)S(1)} %pad_maximum_fusion.5), channel_id=1, source_target_pairs={{0,16},{8,24},{16,0},{24,8},{32,48},{40,56},{48,32},{56,40},{64,80... | collective-permute-start | bytes 331784 | tf_op jit(solution)/shard_map/ppermute | solution.py:47
  158.5 3.5 %pad_slice_fusion.1 = (bf16[1,256,32,64]{1,3,2,0:T(8,128)(2,1)}, bf16[1,256,32,64]{1,3,2,0:T(8,128)(2,1)}, bf16[1,256,32,64]{1,3,2,0:T(8,128)(2,1)}, bf16[1,256,32,64]{1,3,2,0:T(8,128)(2,1)}, bf16[1,256,32,64]{1,3,2,0:T(8,128)(2,1)}) fusion(bf16[3,256,32,64]{1,3,2,0:T(8,128)(2,1)S(1)} %bitcast.399), kind=kLoop, calls=%fused_computation.96 | loop fusion | bytes 8388608 | tf_op jit(solution)/shard_map/slice | solution.py:66
  162.0 9.0 %pad_slice_fusion.2 = (bf16[1,256,32,64]{1,3,2,0:T(8,128)(2,1)S(1)}, bf16[1,256,32,64]{1,3,2,0:T(8,128)(2,1)}, bf16[1,256,32,64]{1,3,2,0:T(8,128)(2,1)}, bf16[1,...) fusion(bf16[3,256,32,64]{1,3,2,0:T(8,128)(2,1)S(1)} %bitcast.400), kind=kLoop, calls=%fused_computation.97 | loop fusion | bytes 23068672 | tf_op jit(solution)/shard_map/slice | solution.py:66
  171.1 3.0 %fusion = f32[32,2048]{1,0:T(8,128)S(1)} fusion(bf16[1,256,2048]{1,2,0:T(8,128)(2,1)} %bitcast.421, bf16[1,256,2048]{1,2,0:T(8,128)(2,1)} %bitcast.420, bf16[1,256,2048]{1,2,0:T(8,128)(2,1)} %bitcast.426, bf16[256,32]{0,1:T(8,128)(2,1)S(1)} %get-tuple-element.79, bf16[256,32]{0,1:T(8,128)(2,1)S(1)} %copy-done.82, bf16[256,32]{0,1:T(8,128)(2,1)S(1)} %copy-done.83), kind=kOutput, calls=%fused_computation.2 | convolution fusion | flops 110247936 | bytes 3457024 | tf_op jit(solution)/shard_map/dcp,co->dop/dot_general | solution.py:80
  183.3 5.4 %collective-permute-done.15 = f32[216,256]{1,0:T(8,128)S(1)} collective-permute-done((f32[216,256]{1,0:T(8,128)S(1)}, f32[216,256]{1,0:T(8,128)S(1)}, u32[]{:S(2)}, u32[]{:S(2)}) %collective-permute-start.15) | collective-permute-done | bytes 221216 | tf_op jit(solution)/shard_map/ppermute | solution.py:47
  191.3 1.7 fusion.56
  (274 shorter events, 36.4 us)
Async XLA Ops:
  7.2 61.2 %all-gather.2.cloned.1.call-start = ((), (), s32[]{:S(2)}) async-start(), calls=%async_computation | async-start | bytes 1179648 | tf_op jit(solution)/shard_map/all_gather | solution.py:111
  7.2 10.3 %collective-permute-start.1 = (bf16[1,32,2048]{2,1,0:T(8,128)(2,1)}, bf16[1,32,2048]{2,1,0:T(8,128)(2,1)S(1)}, u32[]{:S(2)}, u32[]{:S(2)}) collective-permute-start(bf16[1,32,2048]{2,1,0:T(8,128)(2,1)} %param.3), channel_id=1, source_target_pairs={{8,0},{16,8},{24,16},{32,24},{40,32},{48,40},{56,48},{64,56},{72,6... | collective-permute-start | bytes 393224 | tf_op jit(solution)/shard_map/ppermute | solution.py:18
  12.3 5.2 %collective-permute-start = (bf16[1,32,2048]{2,1,0:T(8,128)(2,1)}, bf16[1,32,2048]{2,1,0:T(8,128)(2,1)S(1)}, u32[]{:S(2)}, u32[]{:S(2)}) collective-permute-start(bf16[1,32,2048]{2,1,0:T(8,128)(2,1)} %param.3), channel_id=1, source_target_pairs={{0,8},{8,16},{16,24},{24,32},{32,40},{40,48},{48,56},{56,64},{64,7... | collective-permute-start | bytes 393224 | tf_op jit(solution)/shard_map/ppermute | solution.py:15
  24.8 20.1 %copy-start.13 = (bf16[1,32,32,64]{3,2,1,0:T(8,128)(2,1)S(1)}, bf16[1,32,32,64]{3,2,1,0:T(8,128)(2,1)}, u32[]{:S(2)}) copy-start(bf16[1,32,32,64]{3,2,1,0:T(8,128)(2,1)} %get-tuple-element.35) | copy-start | bytes 393220
  24.8 21.1 %copy-start.12 = (bf16[1,32,32,64]{3,2,1,0:T(8,128)(2,1)S(1)}, bf16[1,32,32,64]{3,2,1,0:T(8,128)(2,1)}, u32[]{:S(2)}) copy-start(bf16[1,32,32,64]{3,2,1,0:T(8,128)(2,1)} %get-tuple-element.36) | copy-start | bytes 393220
  24.8 22.0 %copy-start.11 = (bf16[1,32,32,64]{3,2,1,0:T(8,128)(2,1)S(1)}, bf16[1,32,32,64]{3,2,1,0:T(8,128)(2,1)}, u32[]{:S(2)}) copy-start(bf16[1,32,32,64]{3,2,1,0:T(8,128)(2,1)} %get-tuple-element.37) | copy-start | bytes 393220
  45.9 6.6 %copy-start.35 = (bf16[1,32,2048]{2,1,0:T(8,128)(2,1)S(1)}, bf16[1,32,2048]{2,1,0:T(8,128)(2,1)}, u32[]{:S(2)}) copy-start(bf16[1,32,2048]{2,1,0:T(8,128)(2,1)} %slice.774) | copy-start | bytes 393220
  46.8 5.7 %copy-start.41 = (bf16[1,32,2048]{2,1,0:T(8,128)(2,1)S(1)}, bf16[1,32,2048]{2,1,0:T(8,128)(2,1)}, u32[]{:S(2)}) copy-start(bf16[1,32,2048]{2,1,0:T(8,128)(2,1)} %slice.776) | copy-start | bytes 393220
  48.7 5.4 %copy-start.43 = (bf16[1,32,2048]{2,1,0:T(8,128)(2,1)S(1)}, bf16[1,32,2048]{2,1,0:T(8,128)(2,1)}, u32[]{:S(2)}) copy-start(bf16[1,32,2048]{2,1,0:T(8,128)(2,1)} %slice.783) | copy-start | bytes 393220
  51.4 5.8 %copy-start.37 = (bf16[1,32,2048]{2,1,0:T(8,128)(2,1)}, bf16[1,32,2048]{2,1,0:T(8,128)(2,1)S(1)}, u32[]{:S(2)}) copy-start(bf16[1,32,2048]{2,1,0:T(8,128)(2,1)S(1)} %slice.817) | copy-start | bytes 393220
  51.9 6.3 %copy-start.33 = (bf16[1,32,2048]{2,1,0:T(8,128)(2,1)}, bf16[1,32,2048]{2,1,0:T(8,128)(2,1)S(1)}, u32[]{:S(2)}) copy-start(bf16[1,32,2048]{2,1,0:T(8,128)(2,1)S(1)} %slice.824) | copy-start | bytes 393220
  52.2 6.0 %copy-start.39 = (bf16[1,32,2048]{2,1,0:T(8,128)(2,1)}, bf16[1,32,2048]{2,1,0:T(8,128)(2,1)S(1)}, u32[]{:S(2)}) copy-start(bf16[1,32,2048]{2,1,0:T(8,128)(2,1)S(1)} %slice.826) | copy-start | bytes 393220
  52.5 6.4 %copy-start.31 = (bf16[1,32,2048]{2,1,0:T(8,128)(2,1)}, bf16[1,32,2048]{2,1,0:T(8,128)(2,1)S(1)}, u32[]{:S(2)}) copy-start(bf16[1,32,2048]{2,1,0:T(8,128)(2,1)S(1)} %slice.831) | copy-start | bytes 393220
  52.5 3.1 %copy-start.44 = (bf16[1,32,2048]{2,1,0:T(8,128)(2,1)S(1)}, bf16[1,32,2048]{2,1,0:T(8,128)(2,1)}, u32[]{:S(2)}) copy-start(bf16[1,32,2048]{2,1,0:T(8,128)(2,1)} %slice.792) | copy-start | bytes 393220
  52.5 3.1 %copy-start.47 = (bf16[1,32,2048]{2,1,0:T(8,128)(2,1)S(1)}, bf16[1,32,2048]{2,1,0:T(8,128)(2,1)}, u32[]{:S(2)}) copy-start(bf16[1,32,2048]{2,1,0:T(8,128)(2,1)} %slice.794) | copy-start | bytes 393220
  52.6 3.1 %copy-start.49 = (bf16[1,32,2048]{2,1,0:T(8,128)(2,1)S(1)}, bf16[1,32,2048]{2,1,0:T(8,128)(2,1)}, u32[]{:S(2)}) copy-start(bf16[1,32,2048]{2,1,0:T(8,128)(2,1)} %slice.796) | copy-start | bytes 393220
  52.6 3.1 %copy-start.76 = (bf16[32,256]{1,0:T(8,128)(2,1)S(1)}, bf16[32,256]{1,0:T(8,128)(2,1)}, u32[]{:S(2)}) copy-start(bf16[32,256]{1,0:T(8,128)(2,1)} %get-tuple-element.99) | copy-start | bytes 49156
  52.6 3.1 %copy-start.77 = (bf16[32,256]{1,0:T(8,128)(2,1)S(1)}, bf16[32,256]{1,0:T(8,128)(2,1)}, u32[]{:S(2)}) copy-start(bf16[32,256]{1,0:T(8,128)(2,1)} %get-tuple-element.100) | copy-start | bytes 49156
  52.6 3.1 %copy-start.78 = (bf16[32,256]{1,0:T(8,128)(2,1)S(1)}, bf16[32,256]{1,0:T(8,128)(2,1)}, u32[]{:S(2)}) copy-start(bf16[32,256]{1,0:T(8,128)(2,1)} %get-tuple-element.102) | copy-start | bytes 49156
  59.9 8.4 %copy-start.36 = (bf16[1,32,2048]{2,1,0:T(8,128)(2,1)S(1)}, bf16[1,32,2048]{2,1,0:T(8,128)(2,1)}, u32[]{:S(2)}) copy-start(bf16[1,32,2048]{2,1,0:T(8,128)(2,1)} %slice.774) | copy-start | bytes 393220
  59.9 8.4 %copy-start.42 = (bf16[1,32,2048]{2,1,0:T(8,128)(2,1)S(1)}, bf16[1,32,2048]{2,1,0:T(8,128)(2,1)}, u32[]{:S(2)}) copy-start(bf16[1,32,2048]{2,1,0:T(8,128)(2,1)} %slice.776) | copy-start | bytes 393220
  59.9 8.4 %copy-start.46 = (bf16[1,32,2048]{2,1,0:T(8,128)(2,1)S(1)}, bf16[1,32,2048]{2,1,0:T(8,128)(2,1)}, u32[]{:S(2)}) copy-start(bf16[1,32,2048]{2,1,0:T(8,128)(2,1)} %slice.778) | copy-start | bytes 393220
  61.5 43.7 %collective-permute-start.2 = (f32[1,128,2048]{2,1,0:T(8,128)}, f32[1,128,2048]{2,1,0:T(8,128)}, u32[]{:S(2)}, u32[]{:S(2)}) collective-permute-start(f32[1,128,2048]{2,1,0:T(8,128)} %slice_select_fusion), channel_id=1, source_target_pairs={{0,4},{1,5},{2,6},{3,7},{4,0},{5,1},{6,2},{7,3},{8,12},{9,13},{10,... | collective-permute-start | bytes 3145736 | tf_op jit(solution)/shard_map/ppermute | solution.py:38
  68.3 3.8 %copy-start.14 = (bf16[1,256,2048]{2,1,0:T(8,128)(2,1)S(1)}, bf16[1,256,2048]{2,1,0:T(8,128)(2,1)}, u32[]{:S(2)}) copy-start(bf16[1,256,2048]{2,1,0:T(8,128)(2,1)} %all-gather.2.cloned.1.call-done) | copy-start | bytes 3145732
  70.1 5.2 %copy-start.52 = (bf16[1,32,2048]{2,1,0:T(8,128)(2,1)S(1)}, bf16[1,32,2048]{2,1,0:T(8,128)(2,1)}, u32[]{:S(2)}) copy-start(bf16[1,32,2048]{2,1,0:T(8,128)(2,1)} %param.3) | copy-start | bytes 393220
  70.1 5.2 %copy-start.55 = (bf16[1,32,2048]{2,1,0:T(8,128)(2,1)S(1)}, bf16[1,32,2048]{2,1,0:T(8,128)(2,1)}, u32[]{:S(2)}) copy-start(bf16[1,32,2048]{2,1,0:T(8,128)(2,1)} %copy-done.53) | copy-start | bytes 393220
  70.1 5.2 %copy-start.58 = (bf16[1,32,2048]{2,1,0:T(8,128)(2,1)S(1)}, bf16[1,32,2048]{2,1,0:T(8,128)(2,1)}, u32[]{:S(2)}) copy-start(bf16[1,32,2048]{2,1,0:T(8,128)(2,1)} %copy-done.56) | copy-start | bytes 393220
  72.1 3.7 %copy-start.38 = (bf16[1,32,2048]{2,1,0:T(8,128)(2,1)S(1)}, bf16[1,32,2048]{2,1,0:T(8,128)(2,1)}, u32[]{:S(2)}) copy-start(bf16[1,32,2048]{2,1,0:T(8,128)(2,1)} %copy-done.37) | copy-start | bytes 393220
  76.8 24.3 %copy-start = (bf16[27,32,256]{2,1,0:T(8,128)(2,1)S(1)}, bf16[27,32,256]{2,1,0:T(8,128)(2,1)}, u32[]{:S(2)}) copy-start(bf16[27,32,256]{2,1,0:T(8,128)(2,1)} %param.4) | copy-start | bytes 1327108
  78.9 24.0 %collective-permute-start.7 = (f32[432,256]{1,0:T(8,128)}, f32[432,256]{1,0:T(8,128)}, u32[]{:S(2)}, u32[]{:S(2)}) collective-permute-start(f32[432,256]{1,0:T(8,128)} %slice_select_fusion.2), channel_id=1, source_target_pairs={{0,8},{8,0},{16,24},{24,16},{32,40},{40,32},{48,56},{56,48},{64,72... | collective-permute-start | bytes 1327112 | tf_op jit(solution)/shard_map/ppermute | solution.py:38
  104.1 6.7 %collective-permute-start.8 = (f32[216,256]{1,0:T(8,128)S(1)}, f32[216,256]{1,0:T(8,128)S(1)}, u32[]{:S(2)}, u32[]{:S(2)}) collective-permute-start(f32[216,256]{1,0:T(8,128)S(1)} %slice_select_fusion.4), channel_id=1, source_target_pairs={{0,128},{8,136},{16,144},{24,152},{32,160},{40,168},{48,176},{56,1... | collective-permute-start | bytes 663560 | tf_op jit(solution)/shard_map/ppermute | solution.py:38
  110.8 3.7 %collective-permute-start.9 = (f32[108,256]{1,0:T(8,128)S(1)}, f32[108,256]{1,0:T(8,128)S(1)}, u32[]{:S(2)}, u32[]{:S(2)}) collective-permute-start(f32[108,256]{1,0:T(8,128)S(1)} %slice_select_fusion.5), channel_id=1, source_target_pairs={{0,16},{8,24},{16,0},{24,8},{32,48},{40,56},{48,32},{56,40},{64,80... | collective-permute-start | bytes 331784 | tf_op jit(solution)/shard_map/ppermute | solution.py:38
  112.3 12.6 %collective-permute-start.3 = (f32[1,64,2048]{2,1,0:T(8,128)S(1)}, f32[1,64,2048]{2,1,0:T(8,128)S(1)}, u32[]{:S(2)}, u32[]{:S(2)}) collective-permute-start(f32[1,64,2048]{2,1,0:T(8,128)S(1)} %slice_select_fusion.1), channel_id=1, source_target_pairs={{0,2},{1,3},{2,0},{3,1},{4,6},{5,7},{6,4},{7,5},{8,10},{9,11},{10,... | collective-permute-start | bytes 1572872 | tf_op jit(solution)/shard_map/ppermute | solution.py:38
  114.6 4.0 %collective-permute-start.10 = (f32[54,256]{1,0:T(8,128)S(1)}, f32[54,256]{1,0:T(8,128)S(1)}, u32[]{:S(2)}, u32[]{:S(2)}) collective-permute-start(f32[54,256]{1,0:T(8,128)S(1)} %slice_select_fusion.6), channel_id=1, source_target_pairs={{0,32},{8,40},{16,48},{24,56},{32,0},{40,8},{48,16},{56,24},{64,96... | collective-permute-start | bytes 165896 | tf_op jit(solution)/shard_map/ppermute | solution.py:38
  118.7 7.6 %collective-permute-start.11 = (f32[27,256]{1,0:T(8,128)S(1)}, f32[27,256]{1,0:T(8,128)S(1)}, u32[]{:S(2)}, u32[]{:S(2)}) collective-permute-start(f32[27,256]{1,0:T(8,128)S(1)} %slice_select_fusion.7), channel_id=1, source_target_pairs={{0,64},{8,72},{16,80},{24,88},{32,96},{40,104},{48,112},{56,120},{... | collective-permute-start | bytes 82952 | tf_op jit(solution)/shard_map/ppermute | solution.py:38
  126.3 15.8 %collective-permute-start.12 = (f32[27,256]{1,0:T(8,128)S(1)}, f32[27,256]{1,0:T(8,128)S(1)}, u32[]{:S(2)}, u32[]{:S(2)}) collective-permute-start(f32[27,256]{1,0:T(8,128)S(1)} %select_add_fusion.6), channel_id=1, source_target_pairs={{0,64},{8,72},{16,80},{24,88},{32,96},{40,104},{48,112},{56,120},{... | collective-permute-start | bytes 82952 | tf_op jit(solution)/shard_map/ppermute | solution.py:47
  131.8 12.6 %collective-permute-start.4 = (f32[1,32,2048]{2,1,0:T(8,128)S(1)}, f32[1,32,2048]{2,1,0:T(8,128)S(1)}, u32[]{:S(2)}, u32[]{:S(2)}) collective-permute-start(f32[1,32,2048]{2,1,0:T(8,128)S(1)} %slice_select_fusion.3), channel_id=1, source_target_pairs={{0,1},{1,0},{2,3},{3,2},{4,5},{5,4},{6,7},{7,6},{8,9},{9,8},{10,11... | collective-permute-start | bytes 786440 | tf_op jit(solution)/shard_map/ppermute | solution.py:38
  133.3 23.9 %collective-permute-start.6 = (bf16[1,256,2048]{1,2,0:T(8,128)(2,1)S(1)}, bf16[1,256,2048]{1,2,0:T(8,128)(2,1)S(1)}, u32[]{:S(2)}, u32[]{:S(2)}) collective-permute-start(bf16[1,256,2048]{1,2,0:T(8,128)(2,1)S(1)} %copy.7), channel_id=1, source_target_pairs={{8,0},{16,8},{24,16},{32,24},{40,32},{48,40},{56,48},{64,56},{72,6... | collective-permute-start | bytes 3145736 | tf_op jit(solution)/shard_map/ppermute | solution.py:18
  140.1 17.1 %collective-permute-start.5 = (bf16[1,256,2048]{1,2,0:T(8,128)(2,1)S(1)}, bf16[1,256,2048]{1,2,0:T(8,128)(2,1)S(1)}, u32[]{:S(2)}, u32[]{:S(2)}) collective-permute-start(bf16[1,256,2048]{1,2,0:T(8,128)(2,1)S(1)} %copy.7), channel_id=1, source_target_pairs={{0,8},{8,16},{16,24},{24,32},{32,40},{40,48},{48,56},{56,64},{64,7... | collective-permute-start | bytes 3145736 | tf_op jit(solution)/shard_map/ppermute | solution.py:15
  142.1 12.9 %collective-permute-start.13 = (f32[54,256]{1,0:T(8,128)S(1)}, f32[54,256]{1,0:T(8,128)S(1)}, u32[]{:S(2)}, u32[]{:S(2)}) collective-permute-start(f32[54,256]{1,0:T(8,128)S(1)} %pad_maximum_fusion.6), channel_id=1, source_target_pairs={{0,32},{8,40},{16,48},{24,56},{32,0},{40,8},{48,16},{56,24},{64,96... | collective-permute-start | bytes 165896 | tf_op jit(solution)/shard_map/ppermute | solution.py:47
  155.1 26.6 %collective-permute-start.14 = (f32[108,256]{1,0:T(8,128)S(1)}, f32[108,256]{1,0:T(8,128)S(1)}, u32[]{:S(2)}, u32[]{:S(2)}) collective-permute-start(f32[108,256]{1,0:T(8,128)S(1)} %pad_maximum_fusion.5), channel_id=1, source_target_pairs={{0,16},{8,24},{16,0},{24,8},{32,48},{40,56},{48,32},{56,40},{64,80... | collective-permute-start | bytes 331784 | tf_op jit(solution)/shard_map/ppermute | solution.py:47
  162.0 9.0 %copy-start.82 = (bf16[256,32]{0,1:T(8,128)(2,1)S(1)}, bf16[256,32]{0,1:T(8,128)(2,1)}, u32[]{:S(2)}) copy-start(bf16[256,32]{0,1:T(8,128)(2,1)} %get-tuple-element.80) | copy-start | bytes 49156
  162.0 9.0 %copy-start.83 = (bf16[256,32]{0,1:T(8,128)(2,1)S(1)}, bf16[256,32]{0,1:T(8,128)(2,1)}, u32[]{:S(2)}) copy-start(bf16[256,32]{0,1:T(8,128)(2,1)} %get-tuple-element.81) | copy-start | bytes 49156
  171.0 3.1 %copy-start.8 = (bf16[1,256,32,64]{1,3,2,0:T(8,128)(2,1)S(1)}, bf16[1,256,32,64]{1,3,2,0:T(8,128)(2,1)}, u32[]{:S(2)}) copy-start(bf16[1,256,32,64]{1,3,2,0:T(8,128)(2,1)} %get-tuple-element.15) | copy-start | bytes 3145732
  181.7 7.0 %collective-permute-start.15 = (f32[216,256]{1,0:T(8,128)S(1)}, f32[216,256]{1,0:T(8,128)S(1)}, u32[]{:S(2)}, u32[]{:S(2)}) collective-permute-start(f32[216,256]{1,0:T(8,128)S(1)} %pad_maximum_fusion.4), channel_id=1, source_target_pairs={{0,128},{8,136},{16,144},{24,152},{32,160},{40,168},{48,176},{56,1... | collective-permute-start | bytes 663560 | tf_op jit(solution)/shard_map/ppermute | solution.py:47
  182.3 7.5 %copy-start.21 = (bf16[1,256,32,64]{1,3,2,0:T(8,128)(2,1)S(1)}, bf16[1,256,32,64]{1,3,2,0:T(8,128)(2,1)}, u32[]{:S(2)}) copy-start(bf16[1,256,32,64]{1,3,2,0:T(8,128)(2,1)} %get-tuple-element.23) | copy-start | bytes 3145732
  182.3 7.5 %copy-start.22 = (bf16[1,256,32,64]{1,3,2,0:T(8,128)(2,1)S(1)}, bf16[1,256,32,64]{1,3,2,0:T(8,128)(2,1)}, u32[]{:S(2)}) copy-start(bf16[1,256,32,64]{1,3,2,0:T(8,128)(2,1)} %get-tuple-element.24) | copy-start | bytes 3145732
  188.8 4.2 %collective-permute-start.16 = (f32[432,256]{1,0:T(8,128)S(1)}, f32[432,256]{1,0:T(8,128)S(1)}, u32[]{:S(2)}, u32[]{:S(2)}) collective-permute-start(f32[432,256]{1,0:T(8,128)S(1)} %pad_maximum_fusion.2), channel_id=1, source_target_pairs={{0,8},{8,0},{16,24},{24,16},{32,40},{40,32},{48,56},{56,48},{64,72... | collective-permute-start | bytes 1327112 | tf_op jit(solution)/shard_map/ppermute | solution.py:47
  (54 other events, 73.3 us)
Sparse Core Ops, SparseCore 0:
  14.4 53.8 all-gather.1
